TPU v7x, 32 devices: a whole 2x2x4 slice. The times are simulated.
32 devices in a mesh: blk: 8 (over y, x, core), slab: 4 (over z).
Axes of the slice: x: 2, y: 2, z: 4, core: 2. Of those that a mesh axis runs over, the one named last changes fastest.
Arguments:
- queries: bfloat16 [4096, 4096], P(('blk', 'slab')), may hold values from -8 to 8
- passages: bfloat16 [2816, 4096], P(('blk', 'slab')), may hold values from -6 to 6
- positive: int32 [4096], P(('blk', 'slab')), may hold values from 0 to 703
- hard_ids: int32 [4096, 8], P(('blk', 'slab')), may hold values from 0 to 2815, as said below
Outputs:
- query_loss: float32 [4096], P(('blk', 'slab'))
- query_grad: float32 [4096, 4096], P(('blk', 'slab'))
- passage_grad: float32 [2816, 4096], P(('blk', 'slab'))
Inputs may be any that keep to these rules, and one draw needn't show every extreme that they name: `hard_ids`: passage row f * 88 + t lies on the device of flat index f = b * 4 + s. Of the hard-negative ids of the 128 queries of one device, at most 36 name rows that lie on any one device, and in every draw some device has exactly 36 ids on some one device.
All inputs are finite; a program needn't handle non-finite values.
Results may differ from a plain program's by a relative error of at most 0.008.
Values may be sent and summed in bfloat16 or wider, within the bound.
No kernel may reach another device: no remote copies, remote signals or barrier semaphores. Data moves between devices by JAX's collectives and lax.ppermute only.
A program may use at most 192 MiB of HBM per device.

v0:
```python
import math
import jax
import jax.numpy as jnp
from jax import lax
from jax.sharding import PartitionSpec as P


def per_device(queries, passages, positive, hard_ids):
    slabs = lax.axis_size("slab")
    my_slab = lax.axis_index("slab")
    query_rows_dev, model_width = queries.shape
    passage_rows_dev = passages.shape[0]
    hard_count = hard_ids.shape[1]
    logit_scale = 3.0 / math.sqrt(model_width)
    contract_rows = (((1,), (1,)), ((), ()))
    contract_cols = (((0,), (0,)), ((), ()))
    pool = lax.all_gather(passages, "blk", axis=0, tiled=True)
    pool_size = pool.shape[0]
    column_queries = lax.all_gather(queries, "slab", axis=0, tiled=True)
    column_ids = lax.all_gather(hard_ids, "slab", axis=0, tiled=True)
    column_rows = column_queries.shape[0]
    scores = (
        lax.dot_general(column_queries, pool, contract_rows, preferred_element_type=jnp.float32)
        * logit_scale
    )
    own_start = my_slab * query_rows_dev
    pooled = lax.dynamic_slice_in_dim(scores, own_start, query_rows_dev, axis=0)
    owner_dev = column_ids // passage_rows_dev
    owner_slab = owner_dev % slabs
    hard_pos = owner_dev // slabs * passage_rows_dev + column_ids % passage_rows_dev
    mine = owner_slab == my_slab
    hard_mine = jnp.where(mine, jnp.take_along_axis(scores, hard_pos, axis=1), 0.0)
    pool_max = jnp.max(pooled, axis=1)
    pool_sum = jnp.sum(jnp.exp(pooled - pool_max[:, None]), axis=1)
    payload = jnp.concatenate([hard_mine.reshape(-1), pool_max, pool_sum])
    gathered = lax.all_gather(payload, "slab", axis=0)
    hard_split = column_rows * hard_count
    hard_all = jnp.take_along_axis(
        gathered[:, :hard_split].reshape(slabs, column_rows, hard_count), owner_slab[None], axis=0
    )[0]
    stats = gathered[:, hard_split:].reshape(slabs, 2, query_rows_dev)
    max_all = stats[:, 0].reshape(column_rows)
    sum_all = stats[:, 1].reshape(column_rows)
    row_top = jnp.maximum(max_all, jnp.max(hard_all, axis=1))
    row_total = sum_all * jnp.exp(max_all - row_top) + jnp.sum(
        jnp.exp(hard_all - row_top[:, None]), axis=1
    )
    lse_all = row_top + jnp.log(row_total)
    row_lse = lax.dynamic_slice_in_dim(lse_all, own_start, query_rows_dev)
    onehot = (jnp.arange(pool_size, dtype=jnp.int32)[None, :] == positive[:, None]).astype(
        jnp.float32
    )
    query_loss = row_lse - jnp.sum(onehot * pooled, axis=1)
    coef_pool = (jnp.exp(pooled - row_lse[:, None]) - onehot).astype(jnp.bfloat16)
    coef_hard = jnp.where(
        mine,
        jnp.exp(hard_mine - lse_all[:, None]).astype(jnp.bfloat16),
        jnp.zeros((), jnp.bfloat16),
    )
    hard_matrix = jnp.sum(
        jnp.where(
            hard_pos[:, :, None] == jnp.arange(pool_size, dtype=jnp.int32)[None, None, :],
            coef_hard.astype(jnp.float32)[:, :, None],
            0.0,
        ),
        axis=1,
    ).astype(jnp.bfloat16)
    hard_grad = jnp.dot(hard_matrix, pool, preferred_element_type=jnp.float32).astype(jnp.bfloat16)
    hard_grad = lax.psum_scatter(hard_grad, "slab", scatter_dimension=0, tiled=True)
    pool_grad = jnp.dot(coef_pool, pool, preferred_element_type=jnp.float32)
    query_grad = pool_grad + hard_grad.astype(jnp.float32)
    partial = lax.dot_general(
        coef_pool, queries, contract_cols, preferred_element_type=jnp.float32
    ) + lax.dot_general(
        hard_matrix, column_queries, contract_cols, preferred_element_type=jnp.float32
    )
    passage_grad = lax.psum_scatter(
        partial.astype(jnp.bfloat16), "blk", scatter_dimension=0, tiled=True
    ).astype(jnp.float32)
    return (query_loss, query_grad, passage_grad)


def solution(mesh):
    return jax.shard_map(
        per_device,
        mesh=mesh,
        in_specs=(
            P(("blk", "slab"), None),
            P(("blk", "slab"), None),
            P(("blk", "slab")),
            P(("blk", "slab"), None),
        ),
        out_specs=(P(("blk", "slab")), P(("blk", "slab"), None), P(("blk", "slab"), None)),
        check_vma=False,
    )
```

profile of v0, /device:TPU:0, one launch (start us, length us, event | category | flops | bytes accessed | tf_op | source)
XLA Modules:
  0.0 382.8 jit_solution(10937758230135534292)
XLA Ops:
  7.2 0.7 all-gather.5.cloned.1.call-update
  7.9 0.7 all-gather.7.cloned.1.call-update
  8.7 14.9 %all_gather.15 = s32[512,8]{0,1:T(8,128)S(1)} all-gather(s32[128,8]{0,1:T(8,128)} %param.7), channel_id=1, replica_groups=mesh['blk'=8,'slab'=4] {'slab'}, dimensions={0}, use_global_device_ids=true | all-gather | bytes 20480 | tf_op jit(solution)/shard_map/all_gather | solution.py:20
  23.7 0.1 copy.19
  23.9 0.2 reshape.91
  24.1 0.1 copy.16
  24.2 0.2 reshape.83
  24.3 68.7 %all-gather.5.cloned.1.call-done = bf16[512,4096]{1,0:T(8,128)(2,1)} async-done(((bf16[128,4096]{1,0:T(8,128)(2,1)}), bf16[512,4096]{1,0:T(8,128)(2,1)}) %all-gather.5.cloned.1.call-update) | async-done | bytes 4194320 | tf_op jit(solution)/shard_map/all_gather | solution.py:19
  93.1 43.8 %all-gather.7.cloned.1.call-done = bf16[704,4096]{1,0:T(8,128)(2,1)} async-done(((bf16[88,4096]{1,0:T(8,128)(2,1)}), bf16[704,4096]{1,0:T(8,128)(2,1)}) %all-gather.7.cloned.1.call-update) | async-done | bytes 5767184 | tf_op jit(solution)/shard_map/all_gather | solution.py:17
  136.8 6.5 %convolution_multiply_fusion = f32[512,704]{0,1:T(8,128)S(1)} fusion(bf16[512,4096]{1,0:T(8,128)(2,1)} %all-gather.5.cloned.1.call-done, bf16[704,4096]{1,0:T(8,128)(2,1)} %all-gather.7.cloned.1.call-done), kind=kOutput, calls=%fused_computation.7 | convolution fusion | flops 2953150464 | bytes 11403264 | tf_op jit(solution)/shard_map/dot_general | solution.py:23
  143.3 33.0 %gather_fusion = f32[4096]{0:T(1024)S(1)} fusion(f32[512,704]{0,1:T(8,128)S(1)} %convolution_multiply_fusion, s32[4096]{0:T(1024)S(1)} %reshape.83), kind=kCustom, calls=%fused_computation | custom fusion | bytes 65536 | tf_op jit(solution)/shard_map/jit(take_along_axis)/gather | solution.py:32
  176.4 0.1 dynamic-slice_reduce_fusion
  176.5 0.2 reshape.86
  176.6 0.1 copy.17
  176.8 0.1 copy.18
  176.9 0.2 reshape.79
  177.1 0.1 select_reduce_fusion.1
  177.2 13.3 %all-gather.1 = f32[4,1,4352]{2,1,0:T(1,128)S(1)} all-gather(f32[1,1,4352]{2,1,0:T(1,128)S(1)} %reshape.105), channel_id=2, replica_groups=mesh['blk'=8,'slab'=4] {'slab'}, dimensions={0}, use_global_device_ids=true | all-gather | bytes 87040 | tf_op jit(solution)/shard_map/all_gather | solution.py:36
  190.5 0.6 reshape.81
  191.1 33.1 %gather_fusion.1 = f32[4096]{0:T(1024)S(1)} fusion(f32[4,512,8]{2,1,0:T(8,128)S(1)} %reshape.81, s32[4096]{0:T(1024)S(1)} %reshape.91), kind=kCustom, calls=%fused_computation.1 | custom fusion | bytes 81920 | tf_op jit(solution)/shard_map/jit(take_along_axis)/gather | solution.py:38
  224.3 0.2 gather.12
  224.4 0.1 copy.20
  224.6 1.5 select_reduce_fusion
  226.1 7.6 %convolution_convert_fusion = bf16[512,4096]{1,0:T(8,128)(2,1)} fusion(bf16[704,4096]{1,0:T(8,128)(2,1)} %all-gather.7.cloned.1.call-done, bf16[512,704]{0,1:T(8,128)(2,1)S(1)} %select_reduce_fusion), kind=kOutput, calls=%fused_computation.5 | convolution fusion | flops 2954887168 | bytes 10682368 | tf_op jit(solution)/shard_map/dot_general | solution.py:68
  233.8 0.2 reduce-scatter.5.cloned.1.call-start
  234.0 0.6 fusion.17
  234.6 5.1 %fusion.20 = f32[704,4096]{1,0:T(8,128)S(1)} fusion(bf16[512,704]{0,1:T(8,128)(2,1)S(1)} %select_reduce_fusion, bf16[512,4096]{1,0:T(8,128)(2,1)} %all-gather.5.cloned.1.call-done), kind=kOutput, calls=%fused_computation.57 | convolution fusion | flops 2952790016 | bytes 16449536 | tf_op jit(solution)/shard_map/dot_general | solution.py:74
  239.7 4.2 %add_convert_fusion = bf16[704,4096]{1,0:T(8,128)(2,1)} fusion(f32[704,4096]{1,0:T(8,128)S(1)} %fusion.20, bf16[128,4096]{1,0:T(8,128)(2,1)S(1)} %copy-done, f32[512,704]{0,1:T(8,128)S(1)} %convolution_multiply_fusion, s32[]{:T(128)S(6)} %select_n.62, f32[128]{0:T(128)S(1)} %get-tuple-element.6, s32[128]{0:T(128)S(1)} %copy-done.1), kind=kOutput, calls=%fused_computation.2 | convolution fusion | flops 744415232 | bytes 18711556 | tf_op jit(solution)/shard_map/dot_general | solution.py:72
  244.0 66.7 %reduce-scatter.3.cloned.1.call-done = bf16[128,4096]{1,0:T(8,128)(2,1)} async-done(((bf16[512,4096]{1,0:T(8,128)(2,1)}), bf16[128,4096]{1,0:T(8,128)(2,1)}) %reduce-scatter.3.cloned.1.call-update) | async-done | bytes 1048592 | tf_op jit(solution)/shard_map/reduce_scatter | solution.py:69
  310.6 5.3 %convolution_add_fusion = f32[128,4096]{1,0:T(8,128)} fusion(bf16[704,4096]{1,0:T(8,128)(2,1)} %all-gather.7.cloned.1.call-done, bf16[128,4096]{1,0:T(8,128)(2,1)} %reduce-scatter.3.cloned.1.call-done, f32[512,704]{0,1:T(8,128)S(1)} %convolution_multiply_fusion, s32[]{:T(128)S(6)} %select_n.62, f32[128]{0:T(128)S(1)} %get-tuple-element.6, s32[128]{0:T(128)S(1)} %copy-done.1), kind=kOutput, calls=%fused_computation.6 | convolution fusion | flops 739696640 | bytes 9274372 | tf_op jit(solution)/shard_map/dot_general | solution.py:70
  315.9 58.0 %reduce-scatter.5.cloned.1.call-done = bf16[88,4096]{1,0:T(8,128)(2,1)} async-done(((bf16[704,4096]{1,0:T(8,128)(2,1)}), bf16[88,4096]{1,0:T(8,128)(2,1)}) %reduce-scatter.5.cloned.1.call-update) | async-done | bytes 720912 | tf_op jit(solution)/shard_map/reduce_scatter | solution.py:77
  373.9 2.3 convert_element_type.35
  (28 shorter events, 0.4 us)
Async XLA Ops:
  7.2 85.9 %all-gather.5.cloned.1.call-start = ((), (), s32[]{:S(2)}) async-start(), calls=%async_computation.2 | async-start | bytes 5242880 | tf_op jit(solution)/shard_map/all_gather | solution.py:19
  7.9 128.9 %all-gather.7.cloned.1.call-start = ((), (), s32[]{:S(2)}) async-start(), calls=%async_computation.3 | async-start | bytes 6488064 | tf_op jit(solution)/shard_map/all_gather | solution.py:17
  8.6 302.0 %reduce-scatter.3.cloned.1.call-start = ((), (), s32[]{:S(2)}) async-start(), calls=%async_computation.4 | async-start | bytes 5242880 | tf_op jit(solution)/shard_map/reduce_scatter | solution.py:69
  143.3 33.7 %copy-start.1 = (s32[128]{0:T(128)S(1)}, s32[128]{0:T(128)}, u32[]{:S(2)}) copy-start(s32[128]{0:T(128)} %param.6) | copy-start | bytes 1540
  233.8 140.1 %reduce-scatter.5.cloned.1.call-start = ((), (), s32[]{:S(2)}) async-start(), calls=%async_computation.5 | async-start | bytes 6488064 | tf_op jit(solution)/shard_map/reduce_scatter | solution.py:77
  234.6 5.1 %copy-start = (bf16[128,4096]{1,0:T(8,128)(2,1)S(1)}, bf16[128,4096]{1,0:T(8,128)(2,1)}, u32[]{:S(2)}) copy-start(bf16[128,4096]{1,0:T(8,128)(2,1)} %param.4) | copy-start | bytes 3145732
Sparse Core Ops, SparseCore 0:
  9.6 83.4 all-gather.4
  94.9 41.8 all-gather.6
  233.9 76.6 reduce-scatter.2
  314.3 59.5 reduce-scatter.4
where the time goes:
time: 383 us
  waiting for transfers between devices  239 us (62%)
  local copies, waits for them, and re-layouts  68.1 us (18%)
  matrix products  28.7 us (7%)
  blocking collectives  28.2 us (7%)
  between operations  14 us (4%)
  other arithmetic  4.86 us (1%)
    all_gather x1, waiting for transfers between devices, per_device(): column_queries = lax.all_gather(queries, 'slab', axis=0, tiled=True)  68.7 us
    reduce_scatter x1, waiting for transfers between devices, per_device(): lax.psum_scatter(hard_grad, 'slab', scatter_dimension=0, tiled=True)  66.7 us
    reduce_scatter x1, waiting for transfers between devices, per_device(): lax.psum_scatter(partial.astype(jnp.bfloat16), 'blk', scatter_dimension=0...  58 us
    all_gather x1, waiting for transfers between devices, per_device(): pool = lax.all_gather(passages, 'blk', axis=0, tiled=True)  43.8 us
    gather x5, local copies, waits for them, and re-layouts, per_device(): jnp.take_along_axis(gathered[:, :hard_split].reshape(slabs, column_rows,...  33.6 us
    gather x5, local copies, waits for them, and re-layouts, per_device(): jnp.take_along_axis(scores, hard_pos, axis=1)  33.6 us
    all_gather x1, blocking collectives, per_device(): column_ids = lax.all_gather(hard_ids, 'slab', axis=0, tiled=True)  14.9 us
    all_gather x1, blocking collectives, per_device(): gathered = lax.all_gather(payload, 'slab', axis=0)  13.3 us
  transfers between devices with their start and end apart: 4, of which 4 were waited for; matrix products, arithmetic and copies ran while one was open for 4% of the time, Pallas kernels for 0%

commit v1 on v0

--- a/solution.py
+++ b/solution.py
@@ -16,7 +16,22 @@
     contract_cols = (((0,), (0,)), ((), ()))
     pool = lax.all_gather(passages, "blk", axis=0, tiled=True)
     pool_size = pool.shape[0]
-    column_queries = lax.all_gather(queries, "slab", axis=0, tiled=True)
+    size, here, rows = (lax.axis_size("slab"), lax.axis_index("slab"), queries.shape[0])
+    right = [(i, (i + 1) % size) for i in range(size)]
+    downward = [(i, (i - 1) % size) for i in range(size)]
+    out = jnp.zeros((*queries.shape[:0], size * rows, *queries.shape[0 + 1 :]), queries.dtype)
+    out = lax.dynamic_update_slice_in_dim(out, queries, here * rows, axis=0)
+    from_left = from_right = queries
+    halfway = size // 2
+    for step in range(1, halfway + 1):
+        from_left = lax.ppermute(from_left, "slab", right)
+        out = lax.dynamic_update_slice_in_dim(out, from_left, (here - step) % size * rows, axis=0)
+        if step < size - halfway:
+            from_right = lax.ppermute(from_right, "slab", downward)
+            out = lax.dynamic_update_slice_in_dim(
+                out, from_right, (here + step) % size * rows, axis=0
+            )
+    column_queries = out
     column_ids = lax.all_gather(hard_ids, "slab", axis=0, tiled=True)
     column_rows = column_queries.shape[0]
     scores = (

time: 383 us -> 339 us (0.89)
  waiting for transfers between devices: 239 us -> 145 us
  blocking collectives: 28.2 us -> 66.1 us
  local copies, waits for them, and re-layouts: 68.1 us -> 76.2 us
  starting transfers between devices: 0.34 us -> 5.53 us
    all_gather x1 -> x0, waiting for transfers between devices: 68.7 us -> none  [per_device(): column_queries = lax.all_gather(queries, 'slab', axis=0, tiled=True)]
    all_gather x1, waiting for transfers between devices: 43.8 us -> 0.01 us  [per_device(): pool = lax.all_gather(passages, 'blk', axis=0, tiled=True)]
    all_gather x1, blocking collectives: 14.9 us -> 53 us  [per_device(): column_ids = lax.all_gather(hard_ids, 'slab', axis=0, tiled=True)]
    ppermute x0 -> x3, waiting for transfers between devices: none -> 20 us  [the longest x2 20 us: per_device(): from_left = lax.ppermute(from_left, 'slab', right)]
    ppermute x0 -> x3, starting transfers between devices: none -> 5.23 us  [the longest x2 3.13 us: per_device(): from_left = lax.ppermute(from_left, 'slab', right)]
    dynamic_update_slice x0 -> x4, local copies, waits for them, and re-layouts: none -> 4.64 us  [the longest x1 2.28 us: per_device(): lax.dynamic_update_slice_in_dim(out, from_right, (here + step) % size * r...]
  transfers between devices with their start and end apart: 4 -> 6, of which waited for: 4 -> 3; matrix products, arithmetic and copies ran while one was open for 4% -> 5% of each run, Pallas kernels for 0% -> 0%
where the time goes in v1:
time: 339 us; the launch traced here: 338 us
  waiting for transfers between devices  145 us (43%)
  local copies, waits for them, and re-layouts  76.2 us (22%)
  blocking collectives  66.1 us (19%)
  matrix products  26 us (8%)
  between operations  14.1 us (4%)
  starting transfers between devices  5.53 us (2%)
  other arithmetic  4.86 us (1%)
    reduce_scatter x1, waiting for transfers between devices, per_device(): lax.psum_scatter(hard_grad, 'slab', scatter_dimension=0, tiled=True)  66.5 us
    reduce_scatter x1, waiting for transfers between devices, per_device(): lax.psum_scatter(partial.astype(jnp.bfloat16), 'blk', scatter_dimension=0...  58.1 us
    all_gather x1, blocking collectives, per_device(): column_ids = lax.all_gather(hard_ids, 'slab', axis=0, tiled=True)  53 us
    gather x5, local copies, waits for them, and re-layouts, per_device(): jnp.take_along_axis(gathered[:, :hard_split].reshape(slabs, column_rows,...  33.6 us
    gather x5, local copies, waits for them, and re-layouts, per_device(): jnp.take_along_axis(scores, hard_pos, axis=1)  33.6 us
    ppermute x2, waiting for transfers between devices, per_device(): from_left = lax.ppermute(from_left, 'slab', right)  20 us
    all_gather x1, blocking collectives, per_device(): gathered = lax.all_gather(payload, 'slab', axis=0)  13.2 us
    dot_general x1, matrix products, per_device(): jnp.dot(hard_matrix, pool, preferred_element_type=jnp.float32)  7.64 us
  transfers between devices with their start and end apart: 6, of which 3 were waited for; matrix products, arithmetic and copies ran while one was open for 5% of the time, Pallas kernels for 0%

profile of v1, /device:TPU:0, one launch (start us, length us, event | category | flops | bytes accessed | tf_op | source)
XLA Modules:
  0.0 338.3 jit_solution(10714621083495821996)
XLA Ops:
  7.2 0.7 all-gather.4.cloned.1.call-update
  8.0 3.1 collective-permute-start
  11.0 2.1 collective-permute-start.1
  13.1 53.0 %all_gather.12 = s32[512,8]{0,1:T(8,128)S(1)} all-gather(s32[128,8]{0,1:T(8,128)} %param.7), channel_id=1, replica_groups=mesh['blk'=8,'slab'=4] {'slab'}, dimensions={0}, use_global_device_ids=true | all-gather | bytes 20480 | tf_op jit(solution)/shard_map/all_gather | solution.py:35
  66.1 0.5 broadcast_in_dim.39
  66.8 2.0 copy-done.2
  69.2 0.2 reshape.91
  69.4 0.2 reshape.83
  69.6 1.1 constant_dynamic-update-slice_fusion.2
  70.7 2.3 constant_dynamic-update-slice_fusion.1
  73.0 20.0 %collective-permute-done.2 = bf16[128,4096]{1,0:T(8,128)(2,1)S(1)} collective-permute-done((bf16[128,4096]{1,0:T(8,128)(2,1)S(1)}, bf16[128,4096]{1,0:T(8,128)(2,1)S(1)}, u32[]{:S(2)}, u32[]{:S(2)}) %collective-permute-start.2) | collective-permute-done | bytes 1048608 | tf_op jit(solution)/shard_map/ppermute | solution.py:27
  93.0 1.1 constant_dynamic-update-slice_fusion
  94.2 6.5 %convolution_multiply_fusion = f32[512,704]{0,1:T(8,128)S(1)} fusion(bf16[512,4096]{1,0:T(8,128)(2,1)} %constant_dynamic-update-slice_fusion, bf16[704,4096]{1,0:T(8,128)(2,1)} %all-gather.4.cloned.1.call-done), kind=kOutput, calls=%fused_computation.7 | convolution fusion | flops 2953150464 | bytes 11403264 | tf_op jit(solution)/shard_map/dot_general | solution.py:38
  100.8 33.0 %gather_fusion = f32[4096]{0:T(1024)S(1)} fusion(f32[512,704]{0,1:T(8,128)S(1)} %convolution_multiply_fusion, s32[4096]{0:T(1024)S(1)} %reshape.83), kind=kCustom, calls=%fused_computation | custom fusion | bytes 65536 | tf_op jit(solution)/shard_map/jit(take_along_axis)/gather | solution.py:47
  133.8 0.2 reshape.86
  134.3 0.2 reshape.79
  134.6 13.2 %all-gather.1 = f32[4,1,4352]{2,1,0:T(1,128)S(1)} all-gather(f32[1,1,4352]{2,1,0:T(1,128)S(1)} %reshape.105), channel_id=2, replica_groups=mesh['blk'=8,'slab'=4] {'slab'}, dimensions={0}, use_global_device_ids=true | all-gather | bytes 87040 | tf_op jit(solution)/shard_map/all_gather | solution.py:51
  147.8 0.6 reshape.81
  148.4 33.1 %gather_fusion.1 = f32[4096]{0:T(1024)S(1)} fusion(f32[4,512,8]{2,1,0:T(8,128)S(1)} %reshape.81, s32[4096]{0:T(1024)S(1)} %reshape.91), kind=kCustom, calls=%fused_computation.1 | custom fusion | bytes 81920 | tf_op jit(solution)/shard_map/jit(take_along_axis)/gather | solution.py:53
  181.5 0.2 gather.12
  181.9 1.5 select_reduce_fusion
  183.4 7.6 %convolution_convert_fusion = bf16[512,4096]{1,0:T(8,128)(2,1)} fusion(bf16[704,4096]{1,0:T(8,128)(2,1)} %all-gather.4.cloned.1.call-done, bf16[512,704]{0,1:T(8,128)(2,1)S(1)} %select_reduce_fusion), kind=kOutput, calls=%fused_computation.5 | convolution fusion | flops 2954887168 | bytes 10682368 | tf_op jit(solution)/shard_map/dot_general | solution.py:83
  191.1 0.2 reduce-scatter.5.cloned.1.call-start
  191.3 0.6 fusion.17
  191.9 0.4 copy-done.1
  192.3 1.7 fusion.16
  193.9 0.5 copy-done.3
  194.4 5.0 %add_convert_fusion = bf16[704,4096]{1,0:T(8,128)(2,1)} fusion(f32[704,4096]{1,0:T(8,128)S(1)} %fusion.16, bf16[512,4096]{1,0:T(8,128)(2,1)S(1)} %copy-done.3, bf16[512,704]{0,1:T(8,128)(2,1)S(1)} %select_reduce_fusion), kind=kOutput, calls=%fused_computation.2 | convolution fusion | flops 2958557184 | bytes 22216704 | tf_op jit(solution)/shard_map/dot_general | solution.py:89
  199.5 66.5 %reduce-scatter.3.cloned.1.call-done = bf16[128,4096]{1,0:T(8,128)(2,1)} async-done(((bf16[512,4096]{1,0:T(8,128)(2,1)}), bf16[128,4096]{1,0:T(8,128)(2,1)}) %reduce-scatter.3.cloned.1.call-update) | async-done | bytes 1048592 | tf_op jit(solution)/shard_map/reduce_scatter | solution.py:84
  266.0 5.3 %convolution_add_fusion = f32[128,4096]{1,0:T(8,128)} fusion(bf16[704,4096]{1,0:T(8,128)(2,1)} %all-gather.4.cloned.1.call-done, bf16[128,4096]{1,0:T(8,128)(2,1)} %reduce-scatter.3.cloned.1.call-done, f32[512,704]{0,1:T(8,128)S(1)} %convolution_multiply_fusion, s32[]{:T(128)S(6)} %select_n.84, f32[128]{0:T(128)S(1)} %get-tuple-element.6, s32[128]{0:T(128)S(1)} %copy-done.4), kind=kOutput, calls=%fused_computation.6 | convolution fusion | flops 739696640 | bytes 9274372 | tf_op jit(solution)/shard_map/dot_general | solution.py:85
  271.3 58.1 %reduce-scatter.5.cloned.1.call-done = bf16[88,4096]{1,0:T(8,128)(2,1)} async-done(((bf16[704,4096]{1,0:T(8,128)(2,1)}), bf16[88,4096]{1,0:T(8,128)(2,1)}) %reduce-scatter.5.cloned.1.call-update) | async-done | bytes 720912 | tf_op jit(solution)/shard_map/reduce_scatter | solution.py:92
  329.4 2.3 convert_element_type.35
  (42 shorter events, 1.4 us)
Async XLA Ops:
  7.2 59.5 %copy-start = (bf16[128,4096]{1,0:T(8,128)(2,1)S(1)}, bf16[128,4096]{1,0:T(8,128)(2,1)}, u32[]{:S(2)}) copy-start(bf16[128,4096]{1,0:T(8,128)(2,1)} %param.4) | copy-start | bytes 3145732
  7.2 87.0 %all-gather.4.cloned.1.call-start = ((), (), s32[]{:S(2)}) async-start(), calls=%async_computation.2 | async-start | bytes 6488064 | tf_op jit(solution)/shard_map/all_gather | solution.py:17
  7.9 258.1 %reduce-scatter.3.cloned.1.call-start = ((), (), s32[]{:S(2)}) async-start(), calls=%async_computation.3 | async-start | bytes 5242880 | tf_op jit(solution)/shard_map/reduce_scatter | solution.py:84
  8.0 60.9 %collective-permute-start = (bf16[128,4096]{1,0:T(8,128)(2,1)}, bf16[128,4096]{1,0:T(8,128)(2,1)S(1)}, u32[]{:S(2)}, u32[]{:S(2)}) collective-permute-start(bf16[128,4096]{1,0:T(8,128)(2,1)} %param.4), channel_id=1, source_target_pairs={{0,1},{1,2},{2,3},{3,0},{4,5},{5,6},{6,7},{7,4},{8,9},{9,10},{10,1... | collective-permute-start | bytes 3145736 | tf_op jit(solution)/shard_map/ppermute | solution.py:27
  11.0 59.7 %collective-permute-start.1 = (bf16[128,4096]{1,0:T(8,128)(2,1)}, bf16[128,4096]{1,0:T(8,128)(2,1)}, u32[]{:S(2)}, u32[]{:S(2)}) collective-permute-start(bf16[128,4096]{1,0:T(8,128)(2,1)} %param.4), channel_id=1, source_target_pairs={{0,3},{1,0},{2,1},{3,2},{4,7},{5,4},{6,5},{7,6},{8,11},{9,8},{10,9... | collective-permute-start | bytes 3145736 | tf_op jit(solution)/shard_map/ppermute | solution.py:30
  66.7 2.0 copy-start.2
  68.9 24.2 %collective-permute-start.2 = (bf16[128,4096]{1,0:T(8,128)(2,1)S(1)}, bf16[128,4096]{1,0:T(8,128)(2,1)S(1)}, u32[]{:S(2)}, u32[]{:S(2)}) collective-permute-start(bf16[128,4096]{1,0:T(8,128)(2,1)S(1)} %collective-permute-done), channel_id=1, source_target_pairs={{0,1},{1,2},{2,3},{3,0},{4,5},{5,6},{6,7},{7,4},{8,9},{9,10},{10,1... | collective-permute-start | bytes 3145736 | tf_op jit(solution)/shard_map/ppermute | solution.py:27
  100.8 33.6 %copy-start.4 = (s32[128]{0:T(128)S(1)}, s32[128]{0:T(128)}, u32[]{:S(2)}) copy-start(s32[128]{0:T(128)} %param.6) | copy-start | bytes 1540
  191.0 1.2 copy-start.1
  191.1 138.3 %reduce-scatter.5.cloned.1.call-start = ((), (), s32[]{:S(2)}) async-start(), calls=%async_computation.4 | async-start | bytes 6488064 | tf_op jit(solution)/shard_map/reduce_scatter | solution.py:92
  192.3 2.2 copy-start.3
Sparse Core Ops, SparseCore 0:
  9.9 46.0 all-gather.3
  191.2 74.7 reduce-scatter.2
  269.8 59.5 reduce-scatter.4
